TPU v7x, 128 devices: a whole 4x4x4 slice. The times are simulated.
128 devices in a mesh: row: 8 (over x, y_hi), col: 16 (over y_lo, z, core).
Axes of the slice: x: 4, y: 4 (y_hi: 2, y_lo: 2; y = y_hi * 2 + y_lo), z: 4, core: 2. Of those that a mesh axis runs over, the one named last changes fastest.
Arguments:
- flat_gradient: bfloat16 [8, 16, 524288], P('row', 'col'), may hold values from -6 to 6
- range_rows: int32 [8, 16], replicated, may hold values from 1 to 64, 512 in all within a row
- left_stat: float32 [4096, 4096], P('row', 'col'), may hold values from -6 to 6
- right_stat: float32 [8192, 8192], P('col', 'row'), may hold values from -6 to 6
- left_root: bfloat16 [4096, 4096], P('row'), as said below
- right_root: bfloat16 [8192, 8192], P('col'), as said below
Outputs:
- left_new: float32 [4096, 4096], P('row', 'col')
- right_new: float32 [8192, 8192], P('col', 'row')
- update: bfloat16 [4096, 8192], P('row', 'col')
Inputs may be any that keep to these rules, and one draw needn't show every extreme that they name: In each row r the entries sum to 512; the largest entry of every row is exactly 64. Slots of flat_gradient beyond a device's range_rows rows are padding. left_root equals its transpose. right_root equals its transpose.
All inputs are finite; a program needn't handle non-finite values.
Results may differ from a plain program's by a relative error of at most 0.014.
Values may be sent and summed in bfloat16 or wider, within the bound.
No kernel may reach another device: no remote copies, remote signals or barrier semaphores. Data moves between devices by JAX's collectives and lax.ppermute only.
A program may use at most 192 MiB of HBM per device.

v0:
```python
import math

import jax
import jax.numpy as jnp
from jax import lax
from jax.sharding import PartitionSpec as P

HQ = 4096
DIN = 8192


stat_decay = 0.9


def shifted(block, axis, distance):
    devices = range(lax.axis_size(axis))
    route = [((i - distance) % len(devices), i) for i in devices]
    return lax.ppermute(block, axis, route)


def broadcast(block, axis, source):
    block = jnp.where(lax.axis_index(axis) == source, block, jnp.zeros_like(block))
    return lax.psum(block, axis)


def slot_index(row_counts, tile_rows, capacity):
    offsets = jnp.cumsum(row_counts) - row_counts
    target = jnp.arange(tile_rows, dtype=jnp.int32)
    covered = target[:, None] >= offsets[None, :]
    source = jnp.sum(covered.astype(jnp.int32), axis=1) - 1
    begins = jnp.max(jnp.where(covered, offsets[None, :], 0), axis=1)
    return source * capacity + target - begins


def shards(flat_gradient, range_rows, left_stat, right_stat, left_root, right_root):
    row_count = lax.axis_size("row")
    col_count = lax.axis_size("col")
    row_index = lax.axis_index("row")
    tile_rows = HQ // row_count
    capacity = flat_gradient.shape[2] // DIN
    held_rows = flat_gradient.reshape(capacity, DIN)
    received = lax.all_to_all(held_rows, "col", split_axis=1, concat_axis=0, tiled=True)
    row_counts = lax.dynamic_index_in_dim(range_rows, row_index, 0, keepdims=False)
    grad_tile = jnp.take(received, slot_index(row_counts, tile_rows, capacity), axis=0)
    column_panel = lax.all_gather(grad_tile, "row", axis=0, tiled=True)
    half_count = row_count // 2
    rotated = jnp.roll(column_panel, -row_index * tile_rows, axis=0)
    upper_part = lax.dot_general(
        grad_tile,
        rotated[: (half_count + 1) * tile_rows],
        (((1,), (1,)), ((), ())),
        preferred_element_type=jnp.float32,
    )
    upper_blocks = [
        upper_part[:, stride * tile_rows : (stride + 1) * tile_rows]
        for stride in range(half_count + 1)
    ]
    mirrored = {}
    for stride in range(1, half_count):
        mirrored[stride] = shifted(
            upper_blocks[stride].T.astype(jnp.bfloat16), "row", stride
        ).astype(jnp.float32)
    all_blocks = upper_blocks + [
        mirrored[row_count - distance] for distance in range(half_count + 1, row_count)
    ]
    left_part = jnp.roll(jnp.concatenate(all_blocks, axis=1), row_index * tile_rows, axis=1)
    left_sum = lax.psum_scatter(
        left_part.astype(jnp.bfloat16), "col", scatter_dimension=1, tiled=True
    ).astype(jnp.float32)
    panel_ratio = col_count // row_count
    partner_list = []
    for member in range(panel_ratio):
        partner_list.append(broadcast(column_panel, "col", row_index * panel_ratio + member))
    partner_panel = jnp.concatenate(partner_list, axis=1)
    right_gram = lax.dot_general(
        column_panel, partner_panel, (((0,), (0,)), ((), ())), preferred_element_type=jnp.float32
    )
    right_new = stat_decay * right_stat + right_gram * (1.0 / math.sqrt(HQ))
    left_mixed = jnp.dot(left_root, column_panel, preferred_element_type=jnp.float32).astype(
        jnp.bfloat16
    )
    update_sum = lax.dot_general(
        lax.all_gather(left_mixed, "col", axis=1, tiled=True),
        right_root,
        (((1,), (1,)), ((), ())),
        preferred_element_type=jnp.float32,
    )
    left_new = stat_decay * left_stat + left_sum * (1.0 / math.sqrt(DIN))
    return (left_new, right_new, update_sum.astype(jnp.bfloat16))


def solution(mesh):
    in_specs = (
        P("row", "col", None),
        P(),
        P("row", "col"),
        P("col", "row"),
        P("row", None),
        P("col", None),
    )
    out_specs = (P("row", "col"), P("col", "row"), P("row", "col"))
    return jax.shard_map(shards, mesh=mesh, in_specs=in_specs, out_specs=out_specs, check_vma=False)
```

profile of v0, /device:TPU:1, one launch (start us, length us, event | category | flops | bytes accessed | tf_op | source)
XLA Modules:
  0.0 440.1 jit_solution(12549819292666009770)
XLA Ops:
  7.2 22.8 %reduce = bf16[524288]{0:T(1024)(128)(2,1)S(1)} reduce(bf16[1,1,524288]{2,1,0:T(2,128)(2,1)} %param.6, bf16[]{:T(256)} %constant.91), dimensions={0,1}, to_apply=%param.6.reduce_sub_computation | reduce | bytes 2097154 | tf_op args[0]
  30.6 1.5 copy.13
  32.2 7.8 %all-to-all-start = ((bf16[64,16,512]{2,0,1:T(8,128)(2,1)}), bf16[64,16,512]{2,0,1:T(8,128)(2,1)S(1)}, u32[]{:S(2)}, u32[]{:S(2)}) async-start(bf16[64,16,512]{2,0,1:T(8,128)(2,1)} %copy.13), calls=%async_computation | async-start | bytes 2097152 | tf_op jit(solution)/shard_map/all_to_all | solution.py:42
  41.8 14.0 %all-to-all-done = bf16[64,16,512]{2,0,1:T(8,128)(2,1)S(1)} async-done(((bf16[64,16,512]{2,0,1:T(8,128)(2,1)}), bf16[64,16,512]{2,0,1:T(8,128)(2,1)S(1)}, u32[]{:S(2)}, u32[]{:S(2)}) %all-to-all-start) | async-done | bytes 1048608 | tf_op jit(solution)/shard_map/all_to_all | solution.py:42
  55.9 2.0 gather_fusion
  57.8 0.9 broadcast_select_fusion.2
  58.8 70.9 %all-gather.3.cloned.1.call-done = bf16[4096,512]{1,0:T(8,128)(2,1)} async-done(((bf16[512,512]{1,0:T(8,128)(2,1)}), bf16[4096,512]{1,0:T(8,128)(2,1)}) %all-gather.3.cloned.1.call-update) | async-done | bytes 4194320 | tf_op jit(solution)/shard_map/all_gather | solution.py:45
  129.7 6.0 %broadcast_select_fusion.1 = (bf16[4096,512]{1,0:T(8,128)(2,1)}, bf16[4096,512]{1,0:T(8,128)(2,1)}) fusion(bf16[4096,512]{1,0:T(8,128)(2,1)} %all-gather.3.cloned.1.call-done, pred[]{:T(512)S(6)} %eq.11, pred[]{:T(512)S(6)} %eq.12), kind=kLoop, calls=%fused_computation.9 | loop fusion | flops 4194304 | bytes 12582914 | tf_op jit(solution)/shard_map/jit(_where)/select_n | solution.py:22
  135.8 0.9 copy-done
  136.8 5.1 %constant_dynamic-update-slice_fusion.1 = (bf16[512,8192]{1,0:T(8,128)(2,1)}, bf16[512,2560]{1,0:T(8,128)(2,1)S(1)}) fusion(bf16[512,512]{1,0:T(8,128)(2,1)S(1)} %copy-done, s32[]{:T(128)S(6)} %select_n.71, bf16[4096,512]{1,0:T(8,128)(2,1)} %all-gather.3.cloned.1.call-done), kind=kOutput, calls=%fused_computation.31 | convolution fusion | flops 1347420160 | bytes 9961476 | tf_op jit(solution)/shard_map/dot_general | solution.py:48
  141.9 2.7 copy.14
  144.6 2.5 slice_bitcast_fusion
  147.1 0.8 collective-permute-start.1
  147.9 3.2 collective-permute-start.2
  151.1 12.5 %collective-permute-done = bf16[512,512]{1,0:T(8,128)(2,1)S(1)} collective-permute-done((bf16[512,512]{1,0:T(8,128)(2,1)}, bf16[512,512]{1,0:T(8,128)(2,1)S(1)}, u32[]{:S(2)}, u32[]{:S(2)}) %collective-permute-start) | collective-permute-done | bytes 524320 | tf_op jit(solution)/shard_map/ppermute | solution.py:18
  163.6 0.9 convert_dynamic-update-slice_fusion.4
  164.5 7.7 %collective-permute-done.1 = bf16[512,512]{1,0:T(8,128)(2,1)} collective-permute-done((bf16[512,512]{1,0:T(8,128)(2,1)}, bf16[512,512]{1,0:T(8,128)(2,1)}, u32[]{:S(2)}, u32[]{:S(2)}) %collective-permute-start.1) | collective-permute-done | bytes 524320 | tf_op jit(solution)/shard_map/ppermute | solution.py:18
  172.2 1.9 convert_dynamic-update-slice_fusion.2
  174.1 13.5 %collective-permute-done.2 = bf16[512,512]{1,0:T(8,128)(2,1)S(1)} collective-permute-done((bf16[512,512]{1,0:T(8,128)(2,1)}, bf16[512,512]{1,0:T(8,128)(2,1)S(1)}, u32[]{:S(2)}, u32[]{:S(2)}) %collective-permute-start.2) | collective-permute-done | bytes 524320 | tf_op jit(solution)/shard_map/ppermute | solution.py:18
  187.6 0.8 convert_dynamic-update-slice_fusion
  188.4 1.7 constant_dynamic-update-slice_fusion
  190.1 0.9 convert_dynamic-update-slice_fusion.5
  191.0 2.0 convert_dynamic-update-slice_fusion.3
  193.0 0.9 convert_dynamic-update-slice_fusion.1
  193.9 4.7 %dynamic-slice_convert_fusion = bf16[512,4096]{1,0:T(8,128)(2,1)} fusion(bf16[512,8192]{1,0:T(8,128)(2,1)} %convert_dynamic-update-slice_fusion.1, s32[]{:T(128)S(6)} %select_n.73), kind=kLoop, calls=%fused_computation.7 | loop fusion | bytes 8388612 | tf_op jit(solution)/shard_map/convert_element_type | solution.py:68
  198.6 6.9 %fusion.9 = bf16[512,512]{0,1:T(8,128)(2,1)} fusion(bf16[4096,512]{1,0:T(8,128)(2,1)} %all-gather.3.cloned.1.call-done, bf16[512,4096]{1,0:T(8,128)(2,1)} %param.10), kind=kOutput, calls=%fused_computation.21 | convolution fusion | flops 2147745792 | bytes 8912896 | tf_op jit(solution)/shard_map/dot_general | solution.py:79
  205.5 92.8 %all-reduce.3.cloned.1.call-done = (bf16[4096,512]{1,0:T(8,128)(2,1)}, bf16[4096,512]{1,0:T(8,128)(2,1)}) async-done(((bf16[4096,512]{1,0:T(8,128)(2,1)}, bf16[4096,512]{1,0:T(8,128)(2,1)}), (bf16[4096,512]{1,0:T(8,128)(2,1)}, bf16[4096,512]{1,0:T(8,128)(2,1)})) %all-reduce.3.cloned.1.call-update) | async-done | bytes 8388624 | tf_op jit(solution)/shard_map/psum | solution.py:23
  298.3 10.5 %multiply_add_fusion = f32[512,1024]{1,0:T(8,128)} fusion(f32[512,1024]{1,0:T(8,128)S(1)} %copy-done.2, bf16[4096,512]{1,0:T(8,128)(2,1)} %all-gather.3.cloned.1.call-done, bf16[4096,512]{1,0:T(8,128)(2,1)} %get-tuple-element.5, bf16[4096,512]{1,0:T(8,128)(2,1)} %get-tuple-element.6), kind=kOutput, calls=%fused_computation.12 | convolution fusion | flops 4313317376 | bytes 16777216 | tf_op jit(solution)/shard_map/dot_general | solution.py:75
  308.9 56.4 %reduce-scatter.2.cloned.1.call-done = bf16[512,256]{1,0:T(8,128)(2,1)} async-done(((bf16[512,4096]{1,0:T(8,128)(2,1)}), bf16[512,256]{1,0:T(8,128)(2,1)}) %reduce-scatter.2.cloned.1.call-update) | async-done | bytes 262160 | tf_op jit(solution)/shard_map/reduce_scatter | solution.py:67
  365.3 1.8 multiply_add_fusion.1
  367.1 55.3 %all-gather.5.cloned.1.call-done = bf16[512,8192]{0,1:T(8,128)(2,1)} async-done(((bf16[512,512]{0,1:T(8,128)(2,1)}), bf16[512,8192]{0,1:T(8,128)(2,1)}) %all-gather.5.cloned.1.call-update) | async-done | bytes 8388624 | tf_op jit(solution)/shard_map/all_gather | solution.py:83
  422.5 11.1 %convolution_convert_fusion = bf16[512,512]{1,0:T(8,128)(2,1)} fusion(bf16[512,8192]{0,1:T(8,128)(2,1)} %all-gather.5.cloned.1.call-done, bf16[512,8192]{1,0:T(8,128)(2,1)} %param.11), kind=kOutput, calls=%fused_computation.19 | convolution fusion | flops 4295229440 | bytes 17301504 | tf_op jit(solution)/shard_map/dot_general | solution.py:82
  (23 shorter events, 2.6 us)
Async XLA Ops:
  32.2 23.7 %all-to-all-start = ((bf16[64,16,512]{2,0,1:T(8,128)(2,1)}), bf16[64,16,512]{2,0,1:T(8,128)(2,1)S(1)}, u32[]{:S(2)}, u32[]{:S(2)}) async-start(bf16[64,16,512]{2,0,1:T(8,128)(2,1)} %copy.13), calls=%async_computation | async-start | bytes 2097152 | tf_op jit(solution)/shard_map/all_to_all | solution.py:42
  40.0 89.7 %all-gather.3.cloned.1.call-start = ((), (), s32[]{:S(2)}) async-start(), calls=%async_computation.2 | async-start | bytes 4718592 | tf_op jit(solution)/shard_map/all_gather | solution.py:45
  58.8 239.5 %all-reduce.3.cloned.1.call-start = ((), (), s32[]{:S(2)}) async-start(), calls=%async_computation.5 | async-start | bytes 16777216 | tf_op jit(solution)/shard_map/psum | solution.py:23
  135.7 1.0 copy-start
  135.8 229.5 %reduce-scatter.2.cloned.1.call-start = ((), (), s32[]{:S(2)}) async-start(), calls=%async_computation.3 | async-start | bytes 4456448 | tf_op jit(solution)/shard_map/reduce_scatter | solution.py:67
  147.1 16.5 %collective-permute-start = (bf16[512,512]{1,0:T(8,128)(2,1)}, bf16[512,512]{1,0:T(8,128)(2,1)S(1)}, u32[]{:S(2)}, u32[]{:S(2)}) collective-permute-start(bf16[512,512]{1,0:T(8,128)(2,1)} %get-tuple-element.11), channel_id=1, source_target_pairs={{80,0},{96,16},{112,32},{0,48},{16,64},{32,80},{48,96},{64,112},{8... | collective-permute-start | bytes 1572872 | tf_op jit(solution)/shard_map/ppermute | solution.py:18
  147.1 25.1 %collective-permute-start.1 = (bf16[512,512]{1,0:T(8,128)(2,1)}, bf16[512,512]{1,0:T(8,128)(2,1)}, u32[]{:S(2)}, u32[]{:S(2)}) collective-permute-start(bf16[512,512]{1,0:T(8,128)(2,1)} %get-tuple-element.10), channel_id=1, source_target_pairs={{96,0},{112,16},{0,32},{16,48},{32,64},{48,80},{64,96},{80,112},{9... | collective-permute-start | bytes 1572872 | tf_op jit(solution)/shard_map/ppermute | solution.py:18
  147.9 39.7 %collective-permute-start.2 = (bf16[512,512]{1,0:T(8,128)(2,1)}, bf16[512,512]{1,0:T(8,128)(2,1)S(1)}, u32[]{:S(2)}, u32[]{:S(2)}) collective-permute-start(bf16[512,512]{1,0:T(8,128)(2,1)} %get-tuple-element.9), channel_id=1, source_target_pairs={{112,0},{0,16},{16,32},{32,48},{48,64},{64,80},{80,96},{96,112},{1... | collective-permute-start | bytes 1572872 | tf_op jit(solution)/shard_map/ppermute | solution.py:18
  198.6 99.8 %copy-start.2 = (f32[512,1024]{1,0:T(8,128)S(1)}, f32[512,1024]{1,0:T(8,128)}, u32[]{:S(2)}) copy-start(f32[512,1024]{1,0:T(8,128)} %param.9) | copy-start | bytes 6291460
  198.6 223.9 %all-gather.5.cloned.1.call-start = ((), (), s32[]{:S(2)}) async-start(), calls=%async_computation.4 | async-start | bytes 8912896 | tf_op jit(solution)/shard_map/all_gather | solution.py:83
  298.3 67.0 %copy-start.1 = (f32[512,256]{1,0:T(8,128)S(1)}, f32[512,256]{1,0:T(8,128)}, u32[]{:S(2)}) copy-start(f32[512,256]{1,0:T(8,128)} %param.8) | copy-start | bytes 1572868
Sparse Core Ops, SparseCore 0:
  58.9 70.7 all-gather.2
  135.9 162.4 all-reduce.2
  300.7 64.4 reduce-scatter.1
  367.4 54.9 all-gather.4
where the time goes:
time: 441 us; the launch traced here: 440 us
  waiting for transfers between devices  323 us (73%)
  other arithmetic  40 us (9%)
  matrix products  33.6 us (8%)
  local copies, waits for them, and re-layouts  17.4 us (4%)
  between operations  13.9 us (3%)
  starting transfers between devices  12 us (3%)
    psum x1, waiting for transfers between devices, broadcast(): return lax.psum(block, axis)  92.8 us
    all_gather x1, waiting for transfers between devices, shards(): column_panel = lax.all_gather(grad_tile, 'row', axis=0, tiled=True)  70.9 us
    reduce_scatter x1, waiting for transfers between devices, shards(): lax.psum_scatter(left_part.astype(jnp.bfloat16), 'col', scatter_dimension...  56.4 us
    all_gather x1, waiting for transfers between devices, shards(): lax.all_gather(left_mixed, 'col', axis=1, tiled=True)  55.3 us
    ppermute x3, waiting for transfers between devices, shifted(): return lax.ppermute(block, axis, route)  33.6 us
    unnamed x6, other arithmetic  29.3 us
    all_to_all x1, waiting for transfers between devices, shards(): lax.all_to_all(held_rows, 'col', split_axis=1, concat_axis=0, tiled=True)  14 us
    dot_general x1, matrix products, shards(): lax.dot_general(lax.all_gather(left_mixed, 'col', axis=1, tiled=True), ri...  11.1 us
  transfers between devices with their start and end apart: 8, of which 8 were waited for; matrix products, arithmetic and copies ran while one was open for 10% of the time, Pallas kernels for 0%

commit v1 on v0

v1 whole, which is shorter than its diff:
```python
import math

import jax
import jax.numpy as jnp
from jax import lax
from jax.sharding import PartitionSpec as P

HQ = 4096
DIN = 8192


stat_decay = 0.9


def slot_index(row_counts, tile_rows, capacity):
    offsets = jnp.cumsum(row_counts) - row_counts
    target = jnp.arange(tile_rows, dtype=jnp.int32)
    covered = target[:, None] >= offsets[None, :]
    source = jnp.sum(covered.astype(jnp.int32), axis=1) - 1
    begins = jnp.max(jnp.where(covered, offsets[None, :], 0), axis=1)
    return source * capacity + target - begins


def shards(flat_gradient, range_rows, left_stat, right_stat, left_root, right_root):
    row_count = lax.axis_size("row")
    col_count = lax.axis_size("col")
    row_index = lax.axis_index("row")
    tile_rows = HQ // row_count
    tile_cols = DIN // col_count
    slice_rows = tile_rows // col_count
    block_cols = DIN // row_count
    capacity = flat_gradient.shape[2] // DIN
    held_rows = flat_gradient.reshape(capacity, DIN)
    received = lax.all_to_all(held_rows, "col", split_axis=1, concat_axis=0, tiled=True)
    row_counts = lax.dynamic_index_in_dim(range_rows, row_index, 0, keepdims=False)
    grad_tile = jnp.take(received, slot_index(row_counts, tile_rows, capacity), axis=0)
    row_slice = lax.all_to_all(grad_tile, "col", split_axis=0, concat_axis=1, tiled=True)
    block_piece = lax.all_to_all(row_slice, "row", split_axis=1, concat_axis=0, tiled=True)
    row_block = lax.all_gather(block_piece, "col", axis=0, tiled=True)
    column_panel = lax.all_gather(grad_tile, "row", axis=0, tiled=True)
    left_part = lax.dot_general(
        grad_tile, column_panel, (((1,), (1,)), ((), ())), preferred_element_type=jnp.float32
    )
    left_sum = lax.psum_scatter(
        left_part.astype(jnp.bfloat16), "col", scatter_dimension=1, tiled=True
    ).astype(jnp.float32)
    panel_reordered = (
        column_panel.reshape(row_count, col_count, slice_rows, tile_cols)
        .transpose(1, 0, 2, 3)
        .reshape(HQ, tile_cols)
    )
    right_gram = lax.dot_general(
        panel_reordered, row_block, (((0,), (0,)), ((), ())), preferred_element_type=jnp.float32
    )
    right_new = stat_decay * right_stat + right_gram * (1.0 / math.sqrt(HQ))
    left_mixed = jnp.dot(left_root, column_panel, preferred_element_type=jnp.float32).astype(
        jnp.bfloat16
    )
    update_sum = lax.dot_general(
        lax.all_gather(left_mixed, "col", axis=1, tiled=True),
        right_root,
        (((1,), (1,)), ((), ())),
        preferred_element_type=jnp.float32,
    )
    left_new = stat_decay * left_stat + left_sum * (1.0 / math.sqrt(DIN))
    return (left_new, right_new, update_sum.astype(jnp.bfloat16))


def solution(mesh):
    in_specs = (
        P("row", "col", None),
        P(),
        P("row", "col"),
        P("col", "row"),
        P("row", None),
        P("col", None),
    )
    out_specs = (P("row", "col"), P("col", "row"), P("row", "col"))
    return jax.shard_map(shards, mesh=mesh, in_specs=in_specs, out_specs=out_specs, check_vma=False)
```

time: 441 us -> 335 us (0.76)
  waiting for transfers between devices: 323 us -> 210 us
  blocking collectives: 0 us -> 30.2 us
  other arithmetic: 40 us -> 26.7 us
  local copies, waits for them, and re-layouts: 17.4 us -> 10.7 us
    psum x1 -> x0, waiting for transfers between devices: 92.8 us -> none  [broadcast(): return lax.psum(block, axis)]
    all_gather x0 -> x1, waiting for transfers between devices: none -> 54 us  [shards(): row_block = lax.all_gather(block_piece, 'col', axis=0, tiled=True)]
    ppermute x3 -> x0, waiting for transfers between devices: 33.6 us -> none  [shifted(): return lax.ppermute(block, axis, route)]
    reduce_scatter x1, waiting for transfers between devices: 56.4 us -> 25.9 us  [shards(): lax.psum_scatter(left_part.astype(jnp.bfloat16), 'col', scatter_dimension...]
    all_to_all x0 -> x2, blocking collectives: none -> 30.2 us  [the longest x1 17.6 us: shards(): lax.all_to_all(grad_tile, 'col', split_axis=0, concat_axis=1, tiled=True)]
    all_gather x1, waiting for transfers between devices: 55.3 us -> 44.8 us  [shards(): lax.all_gather(left_mixed, 'col', axis=1, tiled=True)]
    convert_element_type x2 -> x0, local copies, waits for them, and re-layouts: 7.19 us -> none  [the longest x1 4.66 us: shards(): left_part.astype(jnp.bfloat16)]
    unnamed x6 -> x1, other arithmetic: 29.3 us -> 22.8 us
  transfers between devices with their start and end apart: 8 -> 5, of which waited for: 8 -> 5; matrix products, arithmetic and copies ran while one was open for 10% -> 8% of each run, Pallas kernels for 0% -> 0%
where the time goes in v1:
time: 335 us; the launch traced here: 334 us
  waiting for transfers between devices  210 us (63%)
  matrix products  35 us (10%)
  blocking collectives  30.2 us (9%)
  other arithmetic  26.7 us (8%)
  between operations  13.9 us (4%)
  local copies, waits for them, and re-layouts  10.7 us (3%)
  starting transfers between devices  8.19 us (2%)
    all_gather x1, waiting for transfers between devices, shards(): column_panel = lax.all_gather(grad_tile, 'row', axis=0, tiled=True)  70.9 us
    all_gather x1, waiting for transfers between devices, shards(): row_block = lax.all_gather(block_piece, 'col', axis=0, tiled=True)  54 us
    all_gather x1, waiting for transfers between devices, shards(): lax.all_gather(left_mixed, 'col', axis=1, tiled=True)  44.8 us
    reduce_scatter x1, waiting for transfers between devices, shards(): lax.psum_scatter(left_part.astype(jnp.bfloat16), 'col', scatter_dimension...  25.9 us
    unnamed x1, other arithmetic  22.8 us
    all_to_all x1, blocking collectives, shards(): lax.all_to_all(grad_tile, 'col', split_axis=0, concat_axis=1, tiled=True)  17.6 us
    all_to_all x1, waiting for transfers between devices, shards(): lax.all_to_all(held_rows, 'col', split_axis=1, concat_axis=0, tiled=True)  14 us
    all_to_all x1, blocking collectives, shards(): lax.all_to_all(row_slice, 'row', split_axis=1, concat_axis=0, tiled=True)  12.6 us
  transfers between devices with their start and end apart: 5, of which 5 were waited for; matrix products, arithmetic and copies ran while one was open for 8% of the time, Pallas kernels for 0%

profile of v1, /device:TPU:1, one launch (start us, length us, event | category | flops | bytes accessed | tf_op | source)
XLA Modules:
  0.0 334.5 jit_solution(1667419256097028322)
XLA Ops:
  7.2 22.8 %reduce = bf16[524288]{0:T(1024)(128)(2,1)S(1)} reduce(bf16[1,1,524288]{2,1,0:T(2,128)(2,1)} %param.6, bf16[]{:T(256)} %constant.48), dimensions={0,1}, to_apply=%param.6.reduce_sub_computation | reduce | bytes 2097154 | tf_op args[0]
  30.0 0.7 all_to_all.38
  30.6 1.5 copy.23
  32.2 7.8 %all-to-all-start = ((bf16[64,16,512]{2,0,1:T(8,128)(2,1)}), bf16[64,16,512]{2,0,1:T(8,128)(2,1)S(1)}, u32[]{:S(2)}, u32[]{:S(2)}) async-start(bf16[64,16,512]{2,0,1:T(8,128)(2,1)} %copy.23), calls=%async_computation | async-start | bytes 2097152 | tf_op jit(solution)/shard_map/all_to_all | solution.py:34
  40.1 0.7 constant_dynamic-slice_fusion
  40.8 0.2 reduce-window_clone.1
  41.0 0.7 subtract_bitcast_fusion
  41.7 0.1 convert_reduce_fusion
  41.8 14.0 %all-to-all-done = bf16[64,16,512]{2,0,1:T(8,128)(2,1)S(1)} async-done(((bf16[64,16,512]{2,0,1:T(8,128)(2,1)}), bf16[64,16,512]{2,0,1:T(8,128)(2,1)S(1)}, u32[]{:S(2)}, u32[]{:S(2)}) %all-to-all-start) | async-done | bytes 1048608 | tf_op jit(solution)/shard_map/all_to_all | solution.py:34
  55.9 2.0 gather_fusion
  57.8 0.9 broadcast_select_fusion
  58.8 0.0 reduce-scatter.2.cloned.1.call-start
  58.8 70.9 %all-gather.4.cloned.1.call-done = bf16[4096,512]{1,0:T(8,128)(2,1)} async-done(((bf16[512,512]{1,0:T(8,128)(2,1)}), bf16[4096,512]{1,0:T(8,128)(2,1)}) %all-gather.4.cloned.1.call-update) | async-done | bytes 4194320 | tf_op jit(solution)/shard_map/all_gather | solution.py:40
  129.7 6.7 %convolution_convert_fusion = bf16[512,4096]{1,0:T(8,128)(2,1)} fusion(bf16[512,512]{1,0:T(8,128)(2,1)} %broadcast_select_fusion, bf16[4096,512]{1,0:T(8,128)(2,1)} %all-gather.4.cloned.1.call-done), kind=kOutput, calls=%fused_computation.1 | convolution fusion | flops 2149580800 | bytes 8912896 | tf_op jit(solution)/shard_map/dot_general | solution.py:41
  136.5 0.0 all-gather.6.cloned.1.call-start
  136.5 0.1 mul.55
  136.6 0.1 reduce_max.15
  136.7 0.1 broadcast_select_fusion.1
  136.8 17.6 %all_to_all.51 = bf16[16,32,512]{2,1,0:T(8,128)(2,1)S(1)} all-to-all(bf16[16,32,512]{2,1,0:T(8,128)(2,1)S(1)} %broadcast_select_fusion.1), channel_id=1, replica_groups=mesh['row'=8,'col'=16] {'col'}, dimensions={0} | all-to-all | bytes 1048576 | tf_op jit(solution)/shard_map/all_to_all | solution.py:37
  154.4 0.3 copy.25
  154.7 0.2 all_to_all.44
  154.9 0.3 copy.26
  155.2 12.6 %all_to_all.52 = bf16[32,8,1024]{2,0,1:T(8,128)(2,1)} all-to-all(bf16[32,8,1024]{2,0,1:T(8,128)(2,1)S(1)} %copy.26), channel_id=1, replica_groups=mesh['row'=8,'col'=16] {'row'}, dimensions={1} | all-to-all | bytes 1048576 | tf_op jit(solution)/shard_map/all_to_all | solution.py:38
  167.8 0.2 all-gather.8.cloned.1.call-start
  168.0 6.8 %fusion = bf16[512,512]{0,1:T(8,128)(2,1)} fusion(bf16[4096,512]{1,0:T(8,128)(2,1)} %all-gather.4.cloned.1.call-done, bf16[512,4096]{1,0:T(8,128)(2,1)} %param.10), kind=kOutput, calls=%fused_computation.5 | convolution fusion | flops 2147745792 | bytes 8912896 | tf_op jit(solution)/shard_map/dot_general | solution.py:56
  174.8 4.9 %copy.24 = bf16[8,16,32,512]{3,2,0,1:T(8,128)(2,1)} copy(bf16[8,16,32,512]{3,2,1,0:T(8,128)(2,1)} %bitcast.29) | data formatting | bytes 8388608 | tf_op jit(solution)/shard_map/reshape | solution.py:48
  179.8 25.9 %reduce-scatter.2.cloned.1.call-done = bf16[512,256]{1,0:T(8,128)(2,1)} async-done(((bf16[512,4096]{1,0:T(8,128)(2,1)}), bf16[512,256]{1,0:T(8,128)(2,1)}) %reduce-scatter.2.cloned.1.call-update) | async-done | bytes 262160 | tf_op jit(solution)/shard_map/reduce_scatter | solution.py:44
  205.7 1.8 multiply_add_fusion.1
  207.5 54.0 %all-gather.6.cloned.1.call-done = bf16[4096,1024]{1,0:T(8,128)(2,1)} async-done(((bf16[256,1024]{1,0:T(8,128)(2,1)}), bf16[4096,1024]{1,0:T(8,128)(2,1)}) %all-gather.6.cloned.1.call-update) | async-done | bytes 8388624 | tf_op jit(solution)/shard_map/all_gather | solution.py:39
  261.5 10.5 %multiply_add_fusion = f32[512,1024]{1,0:T(8,128)} fusion(f32[512,1024]{1,0:T(8,128)S(1)} %copy-done.1, bf16[4096,512]{1,0:T(8,128)(2,1)} %bitcast.30, bf16[4096,1024]{1,0:T(8,128)(2,1)} %all-gather.6.cloned.1.call-done), kind=kOutput, calls=%fused_computation.2 | convolution fusion | flops 4296540160 | bytes 16777216 | tf_op jit(solution)/shard_map/dot_general | solution.py:52
  272.0 44.8 %all-gather.8.cloned.1.call-done = bf16[512,8192]{0,1:T(8,128)(2,1)} async-done(((bf16[512,512]{0,1:T(8,128)(2,1)}), bf16[512,8192]{0,1:T(8,128)(2,1)}) %all-gather.8.cloned.1.call-update) | async-done | bytes 8388624 | tf_op jit(solution)/shard_map/all_gather | solution.py:60
  316.8 11.1 %convolution_convert_fusion.1 = bf16[512,512]{1,0:T(8,128)(2,1)} fusion(bf16[512,8192]{0,1:T(8,128)(2,1)} %all-gather.8.cloned.1.call-done, bf16[512,8192]{1,0:T(8,128)(2,1)} %param.11), kind=kOutput, calls=%fused_computation.3 | convolution fusion | flops 4295229440 | bytes 17301504 | tf_op jit(solution)/shard_map/dot_general | solution.py:59
  (14 shorter events, 0.2 us)
Async XLA Ops:
  32.2 23.7 %all-to-all-start = ((bf16[64,16,512]{2,0,1:T(8,128)(2,1)}), bf16[64,16,512]{2,0,1:T(8,128)(2,1)S(1)}, u32[]{:S(2)}, u32[]{:S(2)}) async-start(bf16[64,16,512]{2,0,1:T(8,128)(2,1)} %copy.23), calls=%async_computation | async-start | bytes 2097152 | tf_op jit(solution)/shard_map/all_to_all | solution.py:34
  40.0 89.7 %all-gather.4.cloned.1.call-start = ((), (), s32[]{:S(2)}) async-start(), calls=%async_computation.4 | async-start | bytes 4718592 | tf_op jit(solution)/shard_map/all_gather | solution.py:40
  58.8 146.9 %reduce-scatter.2.cloned.1.call-start = ((), (), s32[]{:S(2)}) async-start(), calls=%async_computation.5 | async-start | bytes 4456448 | tf_op jit(solution)/shard_map/reduce_scatter | solution.py:44
  136.5 125.1 %all-gather.6.cloned.1.call-start = ((), (), s32[]{:S(2)}) async-start(), calls=%async_computation.6 | async-start | bytes 8912896 | tf_op jit(solution)/shard_map/all_gather | solution.py:39
  167.8 149.0 %all-gather.8.cloned.1.call-start = ((), (), s32[]{:S(2)}) async-start(), calls=%async_computation.7 | async-start | bytes 8912896 | tf_op jit(solution)/shard_map/all_gather | solution.py:60
  174.8 30.8 %copy-start = (f32[512,256]{1,0:T(8,128)S(1)}, f32[512,256]{1,0:T(8,128)}, u32[]{:S(2)}) copy-start(f32[512,256]{1,0:T(8,128)} %param.8) | copy-start | bytes 1572868
  174.8 86.7 %copy-start.1 = (f32[512,1024]{1,0:T(8,128)S(1)}, f32[512,1024]{1,0:T(8,128)}, u32[]{:S(2)}) copy-start(f32[512,1024]{1,0:T(8,128)} %param.9) | copy-start | bytes 6291460
Sparse Core Ops, SparseCore 0:
  58.9 70.7 all-gather.3
  136.6 69.0 reduce-scatter.1
  207.4 54.1 all-gather.5
  263.7 53.1 all-gather.7
